TPU v7x, 512 devices: a whole 4x8x8 slice. The times are simulated.
512 devices in a mesh: dp: 8 (over y), cls: 64 (over x, z, core).
Axes of the slice: x: 4, y: 8, z: 8, core: 2. Of those that a mesh axis runs over, the one named last changes fastest.
Arguments:
- embeddings: bfloat16 [4608, 4096], P('dp'), may hold values from -128 to 128
- fold_ids: int32 [4608], P('dp'), may hold values from 0 to 4
- labels: int32 [4608], P('dp'), may hold values from 0 to 1023
- weights: bfloat16 [4096, 5120], P('dp', 'cls'), may hold values from -4 to 4
- direction: bfloat16 [4096, 5120], P('dp', 'cls'), may hold values from -0.09375 to 0.09375
Outputs:
- gradient: float32 [4096, 5120], P('dp', 'cls')
- hess_vec: float32 [4096, 5120], P('dp', 'cls')
All inputs are finite; a program needn't handle non-finite values.
Results may differ from a plain program's by a relative error of at most 0.0055.
Values may be sent and summed in bfloat16 or wider, within the bound.
No kernel may reach another device: no remote copies, remote signals or barrier semaphores. Data moves between devices by JAX's collectives and lax.ppermute only.
A program may use at most 64 MiB of HBM per device.

v0:
```python
import jax
import jax.numpy as jnp
from jax import lax
from jax.sharding import PartitionSpec as P

D = 4096
FOLDS = 5


def local(embeddings, fold_ids, labels, weights, direction):
    row_count = embeddings.shape[0]
    columns = weights.shape[1]
    per_class = columns // FOLDS
    logits = jnp.dot(
        embeddings,
        lax.all_gather(weights, "dp", axis=0, tiled=True),
        preferred_element_type=jnp.float32,
    )
    tangent = jnp.dot(
        embeddings,
        lax.all_gather(direction, "dp", axis=0, tiled=True),
        preferred_element_type=jnp.float32,
    )
    logits = logits.reshape(row_count, per_class, FOLDS)
    tangent = tangent.reshape(row_count, per_class, FOLDS)
    local_high = jnp.max(logits, axis=1)
    highest = lax.pmax(local_high, "cls")
    scaled = jnp.exp(logits - highest[:, None, :])
    summed, moment = lax.psum((jnp.sum(scaled, axis=1), jnp.sum(scaled * tangent, axis=1)), "cls")
    probability = scaled / summed[:, None, :]
    mean_tangent = moment / summed
    class_ids = lax.axis_index("cls") * per_class + jnp.arange(per_class, dtype=jnp.int32)
    onehot = (labels[:, None] == class_ids[None, :]).astype(jnp.float32)[:, :, None]
    training = (fold_ids[:, None] != jnp.arange(FOLDS, dtype=jnp.int32)[None, :]).astype(
        jnp.float32
    )[:, None, :]
    residual_rows = (
        (training * (probability - onehot)).reshape(row_count, columns).astype(jnp.bfloat16)
    )
    curvature = (
        (training * probability * (tangent - mean_tangent[:, None, :]))
        .reshape(row_count, columns)
        .astype(jnp.bfloat16)
    )
    contract = (((0,), (0,)), ((), ()))
    share = D // lax.axis_size("dp")
    full_grad, full_hvp = lax.psum(
        (
            lax.dot_general(
                embeddings, residual_rows, contract, preferred_element_type=jnp.float32
            ),
            lax.dot_general(embeddings, curvature, contract, preferred_element_type=jnp.float32),
        ),
        "dp",
    )
    offset = lax.axis_index("dp") * share
    gradient = lax.dynamic_slice_in_dim(full_grad, offset, share, 0)
    hess_vec = lax.dynamic_slice_in_dim(full_hvp, offset, share, 0)
    return (gradient, hess_vec)


def solution(mesh):
    placed = (P("dp", None), P("dp"), P("dp"), P("dp", "cls"), P("dp", "cls"))
    return jax.shard_map(
        local,
        mesh=mesh,
        in_specs=placed,
        out_specs=(P("dp", "cls"), P("dp", "cls")),
        check_vma=False,
    )
```

profile of v0, /device:TPU:2, one launch (start us, length us, event | category | flops | bytes accessed | tf_op | source)
XLA Modules:
  0.0 670.8 jit_solution(5172615857026448851)
XLA Ops:
  7.2 0.0 all-reduce.4.cloned.1.call-start
  7.2 0.7 fusion.1
  7.9 0.8 compare_convert_fusion
  8.8 0.0 copy-start
  8.8 27.7 %all_gather.6 = bf16[4096,80]{0,1:T(8,128)(2,1)S(1)} all-gather(bf16[512,80]{0,1:T(8,128)(2,1)} %param.8), channel_id=1, replica_groups=mesh['dp'=8,'cls'=64] {'dp'}, dimensions={0}, use_global_device_ids=true | all-gather | bytes 737280 | tf_op jit(solution)/shard_map/all_gather | solution.py:16
  36.5 3.9 fusion.2
  40.5 217.1 %pmax.7 = f32[576,5]{0,1:T(8,128)S(1)} all-reduce(f32[576,5]{0,1:T(8,128)S(1)} %reduce_max.9), channel_id=1, replica_groups=mesh['dp'=8,'cls'=64] {'cls'}, use_global_device_ids=true, to_apply=%region_1.0 | all-reduce | flops 2880 | bytes 23040 | tf_op jit(solution)/shard_map/pmax | solution.py:27
  257.7 0.0 copy-done
  257.7 25.8 %all_gather.7 = bf16[4096,80]{0,1:T(8,128)(2,1)S(1)} all-gather(bf16[512,80]{0,1:T(8,128)(2,1)S(1)} %copy-done), channel_id=1, replica_groups=mesh['dp'=8,'cls'=64] {'dp'}, dimensions={0}, use_global_device_ids=true | all-gather | bytes 737280 | tf_op jit(solution)/shard_map/all_gather | solution.py:21
  283.5 3.9 fusion.3
  287.4 0.1 multiply_reduce_fusion
  287.5 246.3 %all-reduce = (f32[576,5]{0,1:T(8,128)S(1)}, f32[576,5]{0,1:T(8,128)S(1)}) all-reduce(f32[576,5]{0,1:T(8,128)S(1)} %get-tuple-element.3, f32[576,5]{0,1:T(8,128)S(1)} %get-tuple-element.2), channel_id=1, replica_groups=mesh['dp'=8,'cls'=64] {'cls'}, use_global_device_ids=true, to_apply=%region_3.0 | all-reduce | flops 5760 | bytes 46080 | tf_op jit(solution)/shard_map/psum | solution.py:29
  533.9 4.5 convolution_bitcast_fusion
  538.4 4.5 convolution_bitcast_fusion.1
  542.9 0.0 all-reduce.4.cloned.1.call-update
  542.9 119.3 %all-reduce.4.cloned.1.call-done = (f32[4096,80]{0,1:T(8,128)}, f32[4096,80]{0,1:T(8,128)}) async-done(((f32[4096,80]{0,1:T(8,128)}, f32[4096,80]{0,1:T(8,128)}), (f32[4096,80]{0,1:T(8,128)}, f32[4096,80]{0,1:T(8,128)})) %all-reduce.4.cloned.1.call-update) | async-done | bytes 2621456 | tf_op jit(solution)/shard_map/psum | solution.py:47
  662.2 1.7 constant_dynamic-slice_fusion
  (15 shorter events, 0.4 us)
Async XLA Ops:
  7.2 655.0 %all-reduce.4.cloned.1.call-start = ((), (), s32[]{:S(2)}) async-start(), calls=%async_computation | async-start | bytes 5242880 | tf_op jit(solution)/shard_map/psum | solution.py:47
  8.8 248.8 %copy-start = (bf16[512,80]{0,1:T(8,128)(2,1)S(1)}, bf16[512,80]{0,1:T(8,128)(2,1)}, u32[]{:S(2)}) copy-start(bf16[512,80]{0,1:T(8,128)(2,1)} %param.9) | copy-start | bytes 245764
Sparse Core Ops, SparseCore 0:
  543.0 119.0 all-reduce.3
where the time goes:
time: 671 us
  blocking collectives  517 us (77%)
  waiting for transfers between devices  119 us (18%)
  matrix products  16.7 us (2%)
  between operations  14.2 us (2%)
    psum x1, blocking collectives, local(): lax.psum((jnp.sum(scaled, axis=1), jnp.sum(scaled * tangent, axis=1)), 'c...  246 us
    pmax x1, blocking collectives, local(): highest = lax.pmax(local_high, 'cls')  217 us
    psum x1, waiting for transfers between devices, local(): lax.psum((lax.dot_general(embeddings, residual_rows, contract, preferred_...  119 us
    all_gather x1, blocking collectives, local(): lax.all_gather(weights, 'dp', axis=0, tiled=True)  27.7 us
    all_gather x1, blocking collectives, local(): lax.all_gather(direction, 'dp', axis=0, tiled=True)  25.8 us
  transfers between devices with their start and end apart: 1, of which 1 were waited for; matrix products, arithmetic and copies ran while one was open for 0% of the time, Pallas kernels for 0%

commit v1 on v0

--- a/solution.py
+++ b/solution.py
@@ -7,14 +7,19 @@
 FOLDS = 5
 
 
+def exchange_gather(value, mesh_axis, d):
+    n_dev = lax.axis_size(mesh_axis)
+    parts = jnp.stack([value for _ in range(n_dev)])
+    parts = lax.all_to_all(parts, mesh_axis, split_axis=0, concat_axis=0)
+    return jnp.concatenate(parts, axis=d)
+
+
 def local(embeddings, fold_ids, labels, weights, direction):
     row_count = embeddings.shape[0]
     columns = weights.shape[1]
     per_class = columns // FOLDS
     logits = jnp.dot(
-        embeddings,
-        lax.all_gather(weights, "dp", axis=0, tiled=True),
-        preferred_element_type=jnp.float32,
+        embeddings, exchange_gather(weights, "dp", 0), preferred_element_type=jnp.float32
     )
     tangent = jnp.dot(
         embeddings,

time: 671 us -> 663 us (0.988)
  blocking collectives: 517 us -> 501 us
  starting transfers between devices: 0.04 us -> 7.27 us
    all_gather x1 -> x0, blocking collectives: 27.7 us -> none  [local(): lax.all_gather(weights, 'dp', axis=0, tiled=True)]
    all_gather x1, blocking collectives: 25.8 us -> 37.7 us  [local(): lax.all_gather(direction, 'dp', axis=0, tiled=True)]
    all_to_all x0 -> x1, starting transfers between devices: none -> 7.23 us  [exchange_gather(): parts = lax.all_to_all(parts, mesh_axis, split_axis=0, concat_axis=0)]
  transfers between devices with their start and end apart: 1 -> 2, of which waited for: 1 -> 1; matrix products, arithmetic and copies ran while one was open for 0% -> 1% of each run, Pallas kernels for 0% -> 0%
where the time goes in v1:
time: 663 us
  blocking collectives  501 us (76%)
  waiting for transfers between devices  119 us (18%)
  matrix products  16.8 us (3%)
  between operations  14.1 us (2%)
  starting transfers between devices  7.27 us (1%)
    psum x1, blocking collectives, local(): lax.psum((jnp.sum(scaled, axis=1), jnp.sum(scaled * tangent, axis=1)), 'c...  246 us
    pmax x1, blocking collectives, local(): highest = lax.pmax(local_high, 'cls')  217 us
    psum x1, waiting for transfers between devices, local(): lax.psum((lax.dot_general(embeddings, residual_rows, contract, preferred_...  119 us
    all_gather x1, blocking collectives, local(): lax.all_gather(direction, 'dp', axis=0, tiled=True)  37.7 us
  transfers between devices with their start and end apart: 2, of which 1 were waited for; matrix products, arithmetic and copies ran while one was open for 1% of the time, Pallas kernels for 0%

profile of v1, /device:TPU:2, one launch (start us, length us, event | category | flops | bytes accessed | tf_op | source)
XLA Modules:
  0.0 662.6 jit_solution(15208722674363858482)
XLA Ops:
  7.2 1.8 stack.2
  8.9 0.0 copy-start.1
  8.9 7.2 %all-to-all-start = ((bf16[8,512,80]{1,2,0:T(8,128)(2,1)}), bf16[8,512,80]{1,2,0:T(8,128)(2,1)S(1)}, u32[]{:S(2)}, u32[]{:S(2)}) async-start(bf16[8,512,80]{1,2,0:T(8,128)(2,1)} %stack.2), calls=%async_computation | async-start | bytes 1310720 | tf_op jit(solution)/shard_map/all_to_all | solution.py:13
  16.2 0.0 all-reduce.4.cloned.1.call-start
  16.2 37.7 %all_gather.3 = bf16[4096,80]{0,1:T(8,128)(2,1)S(1)} all-gather(bf16[512,80]{0,1:T(8,128)(2,1)} %param.9), channel_id=1, replica_groups=mesh['dp'=8,'cls'=64] {'dp'}, dimensions={0}, use_global_device_ids=true | all-gather | bytes 737280 | tf_op jit(solution)/shard_map/all_gather | solution.py:26
  53.9 3.9 fusion.7
  57.9 0.0 copy-done.1
  57.9 0.0 copy-done
  57.9 0.1 compare_convert_fusion
  58.0 0.0 all-to-all-done
  58.0 0.1 copy.24
  58.1 0.3 dot_general.21
  58.3 3.9 fusion.6
  62.2 217.1 %pmax.7 = f32[576,5]{0,1:T(8,128)S(1)} all-reduce(f32[576,5]{0,1:T(8,128)S(1)} %get-tuple-element.10), channel_id=1, replica_groups=mesh['dp'=8,'cls'=64] {'cls'}, use_global_device_ids=true, to_apply=%region_1.0 | all-reduce | flops 2880 | bytes 23040 | tf_op jit(solution)/shard_map/pmax | solution.py:32
  279.3 0.1 multiply_reduce_fusion
  279.4 246.2 %all-reduce = (f32[576,5]{0,1:T(8,128)S(1)}, f32[576,5]{0,1:T(8,128)S(1)}) all-reduce(f32[576,5]{0,1:T(8,128)S(1)} %get-tuple-element.3, f32[576,5]{0,1:T(8,128)S(1)} %get-tuple-element.2), channel_id=1, replica_groups=mesh['dp'=8,'cls'=64] {'cls'}, use_global_device_ids=true, to_apply=%region_3.0 | all-reduce | flops 5760 | bytes 46080 | tf_op jit(solution)/shard_map/psum | solution.py:34
  525.6 0.1 multiply_convert_fusion
  525.8 0.1 convert_element_type.31
  525.9 0.1 convert_element_type.29
  526.0 4.5 convolution_bitcast_fusion.1
  530.5 4.5 convolution_bitcast_fusion
  535.0 0.0 all-reduce.4.cloned.1.call-update
  535.0 119.1 %all-reduce.4.cloned.1.call-done = (f32[4096,80]{0,1:T(8,128)}, f32[4096,80]{0,1:T(8,128)}) async-done(((f32[4096,80]{0,1:T(8,128)}, f32[4096,80]{0,1:T(8,128)}), (f32[4096,80]{0,1:T(8,128)}, f32[4096,80]{0,1:T(8,128)})) %all-reduce.4.cloned.1.call-update) | async-done | bytes 2621456 | tf_op jit(solution)/shard_map/psum | solution.py:52
  654.1 1.7 constant_dynamic-slice_fusion
  (7 shorter events, 0.1 us)
Async XLA Ops:
  8.9 48.9 %copy-start.1 = (s32[576]{0:T(1024)S(1)}, s32[576]{0:T(1024)}, u32[]{:S(2)}) copy-start(s32[576]{0:T(1024)} %param.6) | copy-start | bytes 6916
  8.9 49.0 %copy-start = (s32[576]{0:T(1024)S(1)}, s32[576]{0:T(1024)}, u32[]{:S(2)}) copy-start(s32[576]{0:T(1024)} %param.7) | copy-start | bytes 6916
  8.9 49.0 %all-to-all-start = ((bf16[8,512,80]{1,2,0:T(8,128)(2,1)}), bf16[8,512,80]{1,2,0:T(8,128)(2,1)S(1)}, u32[]{:S(2)}, u32[]{:S(2)}) async-start(bf16[8,512,80]{1,2,0:T(8,128)(2,1)} %stack.2), calls=%async_computation | async-start | bytes 1310720 | tf_op jit(solution)/shard_map/all_to_all | solution.py:13
  16.2 637.9 %all-reduce.4.cloned.1.call-start = ((), (), s32[]{:S(2)}) async-start(), calls=%async_computation.1 | async-start | bytes 5242880 | tf_op jit(solution)/shard_map/psum | solution.py:52
Sparse Core Ops, SparseCore 0:
  535.1 118.8 all-reduce.3
